TPU v7x, 32 devices: a whole 2x2x4 slice. The times are simulated.
32 devices in a mesh: narrow: 8 (over z, x), wide: 4 (over y, core).
Axes of the slice: x: 2, y: 2, z: 4, core: 2. Of those that a mesh axis runs over, the one named last changes fastest.
Arguments:
- amps: bfloat16 [16, 512, 512], P(None, 'narrow', 'wide'), may hold values from -1 to 1
- left_fit: bfloat16 [64, 512, 256], P(None, 'narrow'), may hold values from -0.375 to 0.375
- right_fit: bfloat16 [512, 512, 256], P('narrow', 'wide'), may hold values from -0.375 to 0.375
- pair_list: int32 [16, 2], P('narrow'), may hold values from 0 to 127, as said below
- occ_energy: float32 [128], replicated, may hold values from -2 to -0.5
- vir_energy: float32 [512], replicated, may hold values from 0.5 to 3
Outputs:
- update: float32 [16, 64, 512], P('narrow', None, 'wide')
Inputs may be any that keep to these rules, and one draw needn't show every extreme that they name: `pair_list`: each row (i, j) has i <= j.
All inputs are finite; a program needn't handle non-finite values.
Results may differ from a plain program's by a relative error of at most 0.0029.
Values may be sent and summed in bfloat16 or wider, within the bound.
No kernel may reach another device: no remote copies, remote signals or barrier semaphores. Data moves between devices by JAX's collectives and lax.ppermute only.
A program may use at most 128 MiB of HBM per device.

v0:
```python
import jax
import jax.numpy as jnp
from jax import lax
from jax.sharding import PartitionSpec as P


def body(amps, left_fit, right_fit, pair_list, occ_energy, vir_energy):
    right_all = lax.all_gather(right_fit, "narrow", axis=0, tiled=True)
    vir_total, col_width, aux_width = right_all.shape
    right_mat = right_all.reshape(vir_total, col_width * aux_width)
    rows_total = left_fit.shape[0]
    amps_full = lax.all_to_all(amps, "narrow", split_axis=0, concat_axis=1, tiled=True)
    pairs_here = amps_full.shape[0]
    partials = []
    for start_row in range(0, rows_total, 16):
        row_block = left_fit[start_row : start_row + 16]
        running = jnp.einsum(
            "acq,pcd->padq",
            lax.all_gather(row_block, "narrow", axis=1, tiled=True),
            amps_full,
            preferred_element_type=jnp.float32,
        )
        rows_here = running.shape[1]
        mixed_rows = running.astype(jnp.bfloat16).reshape(
            pairs_here * rows_here, col_width * aux_width
        )
        project_ladder_part = lax.dot_general(
            mixed_rows, right_mat, (((1,), (1,)), ((), ())), preferred_element_type=jnp.float32
        )
        partials.append(project_ladder_part.reshape(pairs_here, rows_here, vir_total))
    reduced = [
        lax.psum_scatter(ladder_part, "wide", scatter_dimension=2, tiled=True)
        for ladder_part in partials
    ]
    ladder_sum = jnp.concatenate(reduced, axis=1)
    local_cols = ladder_sum.shape[2]
    occ_ids = jnp.arange(occ_energy.shape[0], dtype=jnp.int32)
    occ_first = jnp.sum(
        jnp.where(pair_list[:, 0:1] == occ_ids[None, :], occ_energy[None, :], 0.0), axis=1
    )
    occ_second = jnp.sum(
        jnp.where(pair_list[:, 1:2] == occ_ids[None, :], occ_energy[None, :], 0.0), axis=1
    )
    vir_cols = lax.dynamic_slice_in_dim(
        vir_energy, lax.axis_index("wide") * local_cols, local_cols, 0
    )
    vir_rows = vir_energy[:rows_total]
    denominator = (
        (occ_first + occ_second)[:, None, None] - vir_rows[None, :, None] - vir_cols[None, None, :]
    )
    return ladder_sum / denominator


def solution(mesh):
    return jax.shard_map(
        body,
        mesh=mesh,
        in_specs=(
            P(None, "narrow", "wide"),
            P(None, "narrow", None),
            P("narrow", "wide", None),
            P("narrow", None),
            P(),
            P(),
        ),
        out_specs=P("narrow", None, "wide"),
        check_vma=False,
    )
```

profile of v0, /device:TPU:0, one launch (start us, length us, event | category | flops | bytes accessed | tf_op | source)
XLA Modules:
  0.0 1060.1 jit_solution(1422802223781420822)
XLA Ops:
  6.5 0.0 all-gather.14.cloned.1.call-start
  6.5 2.9 fusion.50
  9.4 0.0 all-gather.14.cloned.1.call-update
  9.5 0.0 all-gather.12.cloned.1.call-start
  9.5 0.7 all-gather.12.cloned.1.call-update
  10.2 0.0 all-gather.10.cloned.1.call-start
  10.3 0.7 all-gather.10.cloned.1.call-update
  11.0 0.0 all-gather.6.cloned.1.call-start
  11.0 0.5 all-gather.6.cloned.1.call-update
  11.5 0.0 all-gather.8.cloned.1.call-start
  11.6 6.5 copy.21
  18.1 0.0 copy-start.2
  18.1 0.0 all-gather.8.cloned.1.call-update
  18.1 7.4 all-to-all-start
  25.5 0.0 reduce-scatter.11.cloned.1.call-start
  25.6 0.0 copy-done.2
  25.6 0.1 dynamic_slice.3
  25.7 0.0 copy-done
  25.7 0.2 slice_reduce_fusion
  25.8 0.0 copy-done.1
  25.8 0.2 fusion.49
  26.1 16.1 %all-to-all-done = bf16[16,64,128]{2,1,0:T(8,128)(2,1)S(1)} async-done(((bf16[16,64,128]{2,1,0:T(8,128)(2,1)}), bf16[16,64,128]{2,1,0:T(8,128)(2,1)S(1)}, u32[]{:S(2)}, u32[]{:S(2)}) %all-to-all-start) | async-done | bytes 262176 | tf_op jit(solution)/shard_map/all_to_all | solution.py:12
  42.2 49.1 %all-gather.14.cloned.1.call-done = bf16[16,512,256]{2,1,0:T(8,128)(2,1)} async-done(((bf16[16,64,256]{2,1,0:T(8,128)(2,1)}), bf16[16,512,256]{2,1,0:T(8,128)(2,1)}) %all-gather.14.cloned.1.call-update) | async-done | bytes 4194320 | tf_op jit(solution)/shard_map/all_gather | solution.py:19
  91.2 4.8 convert_bitcast_fusion
  96.0 69.1 %all-gather.12.cloned.1.call-done = bf16[16,512,256]{2,1,0:T(8,128)(2,1)} async-done(((bf16[16,64,256]{2,1,0:T(8,128)(2,1)}), bf16[16,512,256]{2,1,0:T(8,128)(2,1)}) %all-gather.12.cloned.1.call-update) | async-done | bytes 4194320 | tf_op jit(solution)/shard_map/all_gather | solution.py:19
  165.1 4.8 convert_bitcast_fusion.1
  169.9 69.1 %all-gather.10.cloned.1.call-done = bf16[16,512,256]{2,1,0:T(8,128)(2,1)} async-done(((bf16[16,64,256]{2,1,0:T(8,128)(2,1)}), bf16[16,512,256]{2,1,0:T(8,128)(2,1)}) %all-gather.10.cloned.1.call-update) | async-done | bytes 4194320 | tf_op jit(solution)/shard_map/all_gather | solution.py:19
  239.0 4.9 convert_bitcast_fusion.2
  243.8 68.9 %all-gather.6.cloned.1.call-done = bf16[16,512,256]{2,1,0:T(8,128)(2,1)} async-done(((bf16[16,64,256]{2,1,0:T(8,128)(2,1)}), bf16[16,512,256]{2,1,0:T(8,128)(2,1)}) %all-gather.6.cloned.1.call-update) | async-done | bytes 4194320 | tf_op jit(solution)/shard_map/all_gather | solution.py:19
  312.7 3.5 convert_bitcast_fusion.3
  316.2 634.0 %all-gather.8.cloned.1.call-done = bf16[512,128,256]{2,0,1:T(8,128)(2,1)} async-done(((bf16[64,128,256]{2,0,1:T(8,128)(2,1)}), bf16[512,128,256]{2,0,1:T(8,128)(2,1)}) %all-gather.8.cloned.1.call-update) | async-done | bytes 33554448 | tf_op jit(solution)/shard_map/all_gather | solution.py:8
  950.1 16.3 %fusion.43 = f32[2,16,512]{2,1,0:T(8,128)} fusion(bf16[512,128,256]{2,0,1:T(8,128)(2,1)} %all-gather.8.cloned.1.call-done, bf16[2,16,128,256]{3,2,1,0:T(8,128)(2,1)} %convert_bitcast_fusion), kind=kOutput, calls=%fused_computation.27 | convolution fusion | flops 1073741824 | bytes 35717120 | tf_op jit(solution)/shard_map/dot_general | solution.py:27
  966.4 0.0 reduce-scatter.11.cloned.1.call-update
  966.4 0.0 reduce-scatter.9.cloned.1.call-start
  966.5 16.3 %fusion.38 = f32[2,16,512]{2,1,0:T(8,128)} fusion(bf16[512,128,256]{2,0,1:T(8,128)(2,1)} %all-gather.8.cloned.1.call-done, bf16[2,16,128,256]{3,2,1,0:T(8,128)(2,1)} %convert_bitcast_fusion.1), kind=kOutput, calls=%fused_computation.26 | convolution fusion | flops 1073741824 | bytes 35717120 | tf_op jit(solution)/shard_map/dot_general | solution.py:27
  982.8 0.0 reduce-scatter.9.cloned.1.call-update
  982.8 0.2 reduce-scatter.7.cloned.1.call-start
  983.0 16.3 %fusion.33 = f32[2,16,512]{2,1,0:T(8,128)} fusion(bf16[512,128,256]{2,0,1:T(8,128)(2,1)} %all-gather.8.cloned.1.call-done, bf16[2,16,128,256]{3,2,1,0:T(8,128)(2,1)} %convert_bitcast_fusion.2), kind=kOutput, calls=%fused_computation.25 | convolution fusion | flops 1073741824 | bytes 35717120 | tf_op jit(solution)/shard_map/dot_general | solution.py:27
  999.4 0.0 reduce-scatter.7.cloned.1.call-update
  999.4 0.0 slice-start
  999.4 0.0 reduce-scatter.5.cloned.1.call-start
  999.4 15.9 %fusion.28 = f32[2,16,512]{2,1,0:T(8,128)} fusion(bf16[512,128,256]{2,0,1:T(8,128)(2,1)} %all-gather.8.cloned.1.call-done, bf16[2,16,128,256]{3,2,1,0:T(8,128)(2,1)S(1)} %convert_bitcast_fusion.3), kind=kOutput, calls=%fused_computation.24 | convolution fusion | flops 1073741824 | bytes 35717120 | tf_op jit(solution)/shard_map/dot_general | solution.py:27
  1015.3 0.0 reduce-scatter.5.cloned.1.call-update
  1015.4 0.0 slice-done
  1015.4 0.1 broadcast_subtract_fusion
  1015.5 14.6 %reduce-scatter.7.cloned.1.call-done = f32[2,16,128]{2,1,0:T(8,128)} async-done(((f32[2,16,512]{2,1,0:T(8,128)}), f32[2,16,128]{2,1,0:T(8,128)}) %reduce-scatter.7.cloned.1.call-update) | async-done | bytes 16400 | tf_op jit(solution)/shard_map/reduce_scatter | solution.py:32
  1030.0 22.0 %reduce-scatter.5.cloned.1.call-done = f32[2,16,128]{2,1,0:T(8,128)} async-done(((f32[2,16,512]{2,1,0:T(8,128)}), f32[2,16,128]{2,1,0:T(8,128)}) %reduce-scatter.5.cloned.1.call-update) | async-done | bytes 16400 | tf_op jit(solution)/shard_map/reduce_scatter | solution.py:32
  1052.1 1.5 maximum_divide_fusion
  (6 shorter events, 0.0 us)
Async XLA Ops:
  6.5 84.7 %all-gather.14.cloned.1.call-start = ((), (), s32[]{:S(2)}) async-start(), calls=%async_computation.12 | async-start | bytes 4718592 | tf_op jit(solution)/shard_map/all_gather | solution.py:19
  9.5 155.6 %all-gather.12.cloned.1.call-start = ((), (), s32[]{:S(2)}) async-start(), calls=%async_computation.10 | async-start | bytes 4718592 | tf_op jit(solution)/shard_map/all_gather | solution.py:19
  10.2 228.8 %all-gather.10.cloned.1.call-start = ((), (), s32[]{:S(2)}) async-start(), calls=%async_computation.8 | async-start | bytes 4718592 | tf_op jit(solution)/shard_map/all_gather | solution.py:19
  11.0 301.7 %all-gather.6.cloned.1.call-start = ((), (), s32[]{:S(2)}) async-start(), calls=%async_computation.5 | async-start | bytes 4718592 | tf_op jit(solution)/shard_map/all_gather | solution.py:19
  11.5 938.6 %all-gather.8.cloned.1.call-start = ((), (), s32[]{:S(2)}) async-start(), calls=%async_computation.6 | async-start | bytes 37748736 | tf_op jit(solution)/shard_map/all_gather | solution.py:8
  18.1 7.5 copy-start.2
  18.1 7.6 copy-start
  18.1 7.7 copy-start.1
  18.1 24.0 %all-to-all-start = ((bf16[16,64,128]{2,1,0:T(8,128)(2,1)}), bf16[16,64,128]{2,1,0:T(8,128)(2,1)S(1)}, u32[]{:S(2)}, u32[]{:S(2)}) async-start(bf16[16,64,128]{2,1,0:T(8,128)(2,1)} %param.6), calls=%async_computation | async-start | bytes 524288 | tf_op jit(solution)/shard_map/all_to_all | solution.py:12
  25.5 989.9 %reduce-scatter.11.cloned.1.call-start = ((), (), s32[]{:S(2)}) async-start(), calls=%async_computation.13 | async-start | bytes 81920 | tf_op jit(solution)/shard_map/reduce_scatter | solution.py:32
  966.4 49.0 %reduce-scatter.9.cloned.1.call-start = ((), (), s32[]{:S(2)}) async-start(), calls=%async_computation.11 | async-start | bytes 81920 | tf_op jit(solution)/shard_map/reduce_scatter | solution.py:32
  982.8 47.2 %reduce-scatter.7.cloned.1.call-start = ((), (), s32[]{:S(2)}) async-start(), calls=%async_computation.9 | async-start | bytes 81920 | tf_op jit(solution)/shard_map/reduce_scatter | solution.py:32
  999.4 16.0 %slice-start = ((f32[512]{0:T(512)}), f32[64]{0:T(128)S(1)}, s32[]{:S(2)}) async-start(f32[512]{0:T(512)} %param.11), calls=%async_computation.14 | async-start | bytes 1024 | tf_op jit(solution)/shard_map/slice | solution.py:47
  999.4 52.7 %reduce-scatter.5.cloned.1.call-start = ((), (), s32[]{:S(2)}) async-start(), calls=%async_computation.7 | async-start | bytes 81920 | tf_op jit(solution)/shard_map/reduce_scatter | solution.py:32
Sparse Core Ops, SparseCore 0:
  9.6 81.6 all-gather.13
  93.4 71.6 all-gather.11
  167.3 71.6 all-gather.9
  241.0 71.6 all-gather.5
  314.1 635.9 all-gather.7
  966.5 19.4 reduce-scatter.10
  988.6 19.4 reduce-scatter.8
  1010.5 19.5 reduce-scatter.6
  1032.6 19.4 reduce-scatter.4
where the time goes:
time: 1060 us
  waiting for transfers between devices  945 us (89%)
  matrix products  82.7 us (8%)
  between operations  13.3 us (1%)
    all_gather x1, waiting for transfers between devices, body(): right_all = lax.all_gather(right_fit, 'narrow', axis=0, tiled=True)  634 us
    all_gather x4, waiting for transfers between devices, body(): lax.all_gather(row_block, 'narrow', axis=1, tiled=True)  256 us
    dot_general x4, matrix products, body(): lax.dot_general(mixed_rows, right_mat, (((1,), (1,)), ((), ())), preferre...  64.8 us
    reduce_scatter x4, waiting for transfers between devices, body(): lax.psum_scatter(ladder_part, 'wide', scatter_dimension=2, tiled=True)  36.6 us
  transfers between devices with their start and end apart: 10, of which 8 were waited for; matrix products, arithmetic and copies ran while one was open for 7% of the time, Pallas kernels for 0%

commit v1 on v0

--- a/solution.py
+++ b/solution.py
@@ -2,6 +2,27 @@
 import jax.numpy as jnp
 from jax import lax
 from jax.sharding import PartitionSpec as P
+
+
+def collect(value, axis, dim):
+    size, index, span = (lax.axis_size(axis), lax.axis_index(axis), value.shape[dim])
+    ahead = [(i, (i + 1) % size) for i in range(size)]
+    backward = [(i, (i - 1) % size) for i in range(size)]
+    result = jnp.zeros((*value.shape[:dim], size * span, *value.shape[dim + 1 :]), value.dtype)
+    result = lax.dynamic_update_slice_in_dim(result, value, index * span, axis=dim)
+    from_left = from_right = value
+    half = size // 2
+    for hop in range(1, half + 1):
+        from_left = lax.ppermute(from_left, axis, ahead)
+        result = lax.dynamic_update_slice_in_dim(
+            result, from_left, (index - hop) % size * span, axis=dim
+        )
+        if hop < size - half:
+            from_right = lax.ppermute(from_right, axis, backward)
+            result = lax.dynamic_update_slice_in_dim(
+                result, from_right, (index + hop) % size * span, axis=dim
+            )
+    return result
 
 
 def body(amps, left_fit, right_fit, pair_list, occ_energy, vir_energy):
@@ -16,7 +37,7 @@
         row_block = left_fit[start_row : start_row + 16]
         running = jnp.einsum(
             "acq,pcd->padq",
-            lax.all_gather(row_block, "narrow", axis=1, tiled=True),
+            collect(row_block, "narrow", 1),
             amps_full,
             preferred_element_type=jnp.float32,
         )

time: 1060 us -> 1150 us (1.085)
  local copies, waits for them, and re-layouts: 9.72 us -> 421 us
  waiting for transfers between devices: 945 us -> 573 us
  starting transfers between devices: 7.9 us -> 47.2 us
    all_gather x1, waiting for transfers between devices: 634 us -> 0.01 us  [body(): right_all = lax.all_gather(right_fit, 'narrow', axis=0, tiled=True)]
    ppermute x0 -> x28, waiting for transfers between devices: none -> 505 us  [the longest x16 408 us: collect(): from_left = lax.ppermute(from_left, axis, ahead)]
    dynamic_update_slice x0 -> x32, local copies, waits for them, and re-layouts: none -> 355 us  [the longest x16 174 us: collect(): lax.dynamic_update_slice_in_dim(result, from_left, (index - hop) % size *...]
    all_gather x4 -> x0, waiting for transfers between devices: 256 us -> none  [body(): lax.all_gather(row_block, 'narrow', axis=1, tiled=True)]
    ppermute x0 -> x28, starting transfers between devices: none -> 30.9 us  [the longest x12 18.8 us: collect(): from_right = lax.ppermute(from_right, axis, backward)]
    ppermute x0 -> x28, local copies, waits for them, and re-layouts: none -> 27 us  [the longest x16 17.1 us: collect(): from_left = lax.ppermute(from_left, axis, ahead)]
    convert_element_type x0 -> x4, local copies, waits for them, and re-layouts: none -> 15.4 us  [body(): running.astype(jnp.bfloat16)]
  transfers between devices with their start and end apart: 10 -> 34, of which waited for: 8 -> 25; matrix products, arithmetic and copies ran while one was open for 7% -> 42% of each run, Pallas kernels for 0% -> 0%
where the time goes in v1:
time: 1150 us; the launch traced here: 1140 us
  waiting for transfers between devices  573 us (50%)
  local copies, waits for them, and re-layouts  421 us (37%)
  matrix products  81.9 us (7%)
  starting transfers between devices  47.2 us (4%)
  between operations  14 us (1%)
    ppermute x16, waiting for transfers between devices, collect(): from_left = lax.ppermute(from_left, axis, ahead)  408 us
    dynamic_update_slice x16, local copies, waits for them, and re-layouts, collect(): lax.dynamic_update_slice_in_dim(result, from_left, (index - hop) % size *...  174 us
    dynamic_update_slice x12, local copies, waits for them, and re-layouts, collect(): lax.dynamic_update_slice_in_dim(result, from_right, (index + hop) % size...  139 us
    ppermute x12, waiting for transfers between devices, collect(): from_right = lax.ppermute(from_right, axis, backward)  97.1 us
    dot_general x4, matrix products, body(): lax.dot_general(mixed_rows, right_mat, (((1,), (1,)), ((), ())), preferre...  64.2 us
    reduce_scatter x4, waiting for transfers between devices, body(): lax.psum_scatter(ladder_part, 'wide', scatter_dimension=2, tiled=True)  43.8 us
    dynamic_update_slice x4, local copies, waits for them, and re-layouts, collect(): lax.dynamic_update_slice_in_dim(result, value, index * span, axis=dim)  41.6 us
    all_to_all x1, waiting for transfers between devices, body(): lax.all_to_all(amps, 'narrow', split_axis=0, concat_axis=1, tiled=True)  23.8 us
  transfers between devices with their start and end apart: 34, of which 25 were waited for; matrix products, arithmetic and copies ran while one was open for 42% of the time, Pallas kernels for 0%

profile of v1, /device:TPU:0, one launch (start us, length us, event | category | flops | bytes accessed | tf_op | source)
XLA Modules:
  0.0 1139.0 jit_solution(15816928569361012489)
XLA Ops:
  25.9 87.0 %collective-permute-done = bf16[16,64,256]{2,1,0:T(8,128)(2,1)S(1)} collective-permute-done((bf16[16,64,256]{2,1,0:T(8,128)(2,1)S(1)}, bf16[16,64,256]{2,1,0:T(8,128)(2,1)S(1)}, u32[]{:S(2)}, u32[]{:S(2)}) %collective-permute-start) | collective-permute-done | bytes 524320 | tf_op jit(solution)/shard_map/ppermute | solution.py:16
  122.6 35.3 %collective-permute-done.7 = bf16[16,64,256]{2,1,0:T(8,128)(2,1)S(1)} collective-permute-done((bf16[16,64,256]{2,1,0:T(8,128)(2,1)S(1)}, bf16[16,64,256]{2,1,0:T(8,128)(2,1)S(1)}, u32[]{:S(2)}, u32[]{:S(2)}) %collective-permute-start.7) | collective-permute-done | bytes 524320 | tf_op jit(solution)/shard_map/ppermute | solution.py:16
  167.5 35.3 %collective-permute-done.14 = bf16[16,64,256]{2,1,0:T(8,128)(2,1)S(1)} collective-permute-done((bf16[16,64,256]{2,1,0:T(8,128)(2,1)S(1)}, bf16[16,64,256]{2,1,0:T(8,128)(2,1)S(1)}, u32[]{:S(2)}, u32[]{:S(2)}) %collective-permute-start.14) | collective-permute-done | bytes 524320 | tf_op jit(solution)/shard_map/ppermute | solution.py:16
  212.4 35.3 %collective-permute-done.21 = bf16[16,64,256]{2,1,0:T(8,128)(2,1)S(1)} collective-permute-done((bf16[16,64,256]{2,1,0:T(8,128)(2,1)S(1)}, bf16[16,64,256]{2,1,0:T(8,128)(2,1)S(1)}, u32[]{:S(2)}, u32[]{:S(2)}) %collective-permute-start.21) | collective-permute-done | bytes 524320 | tf_op jit(solution)/shard_map/ppermute | solution.py:16
  257.4 35.2 %collective-permute-done.2 = bf16[16,64,256]{2,1,0:T(8,128)(2,1)S(1)} collective-permute-done((bf16[16,64,256]{2,1,0:T(8,128)(2,1)S(1)}, bf16[16,64,256]{2,1,0:T(8,128)(2,1)S(1)}, u32[]{:S(2)}, u32[]{:S(2)}) %collective-permute-start.2) | collective-permute-done | bytes 524320 | tf_op jit(solution)/shard_map/ppermute | solution.py:16
  302.3 35.3 %collective-permute-done.9 = bf16[16,64,256]{2,1,0:T(8,128)(2,1)S(1)} collective-permute-done((bf16[16,64,256]{2,1,0:T(8,128)(2,1)S(1)}, bf16[16,64,256]{2,1,0:T(8,128)(2,1)S(1)}, u32[]{:S(2)}, u32[]{:S(2)}) %collective-permute-start.9) | collective-permute-done | bytes 524320 | tf_op jit(solution)/shard_map/ppermute | solution.py:16
  347.3 35.3 %collective-permute-done.16 = bf16[16,64,256]{2,1,0:T(8,128)(2,1)S(1)} collective-permute-done((bf16[16,64,256]{2,1,0:T(8,128)(2,1)S(1)}, bf16[16,64,256]{2,1,0:T(8,128)(2,1)S(1)}, u32[]{:S(2)}, u32[]{:S(2)}) %collective-permute-start.16) | collective-permute-done | bytes 524320 | tf_op jit(solution)/shard_map/ppermute | solution.py:16
  392.3 35.2 %collective-permute-done.23 = bf16[16,64,256]{2,1,0:T(8,128)(2,1)} collective-permute-done((bf16[16,64,256]{2,1,0:T(8,128)(2,1)S(1)}, bf16[16,64,256]{2,1,0:T(8,128)(2,1)}, u32[]{:S(2)}, u32[]{:S(2)}) %collective-permute-start.23) | collective-permute-done | bytes 524320 | tf_op jit(solution)/shard_map/ppermute | solution.py:16
  427.5 9.8 collective-permute-done.24
  437.3 29.6 %collective-permute-done.4 = bf16[16,64,256]{2,1,0:T(8,128)(2,1)} collective-permute-done((bf16[16,64,256]{2,1,0:T(8,128)(2,1)S(1)}, bf16[16,64,256]{2,1,0:T(8,128)(2,1)}, u32[]{:S(2)}, u32[]{:S(2)}) %collective-permute-start.4) | collective-permute-done | bytes 524320 | tf_op jit(solution)/shard_map/ppermute | solution.py:16
  482.1 29.7 %collective-permute-done.11 = bf16[16,64,256]{2,1,0:T(8,128)(2,1)} collective-permute-done((bf16[16,64,256]{2,1,0:T(8,128)(2,1)S(1)}, bf16[16,64,256]{2,1,0:T(8,128)(2,1)}, u32[]{:S(2)}, u32[]{:S(2)}) %collective-permute-start.11) | collective-permute-done | bytes 524320 | tf_op jit(solution)/shard_map/ppermute | solution.py:16
  527.8 16.1 %all-to-all-start = ((bf16[16,64,128]{2,1,0:T(8,128)(2,1)}), bf16[16,64,128]{2,1,0:T(8,128)(2,1)S(1)}, u32[]{:S(2)}, u32[]{:S(2)}) async-start(bf16[16,64,128]{2,1,0:T(8,128)(2,1)} %param.6), calls=%async_computation | async-start | bytes 524288 | tf_op jit(solution)/shard_map/all_to_all | solution.py:33
  544.0 15.3 %collective-permute-done.18 = bf16[16,64,256]{2,1,0:T(8,128)(2,1)} collective-permute-done((bf16[16,64,256]{2,1,0:T(8,128)(2,1)S(1)}, bf16[16,64,256]{2,1,0:T(8,128)(2,1)}, u32[]{:S(2)}, u32[]{:S(2)}) %collective-permute-start.18) | collective-permute-done | bytes 524320 | tf_op jit(solution)/shard_map/ppermute | solution.py:16
  568.6 10.8 dynamic_update_slice.96
  581.8 10.3 dynamic_update_slice.104
  594.5 10.2 dynamic_update_slice.112
  607.1 10.3 dynamic_update_slice.120
  617.7 23.8 %all-to-all-done = bf16[16,64,128]{2,1,0:T(8,128)(2,1)S(1)} async-done(((bf16[16,64,128]{2,1,0:T(8,128)(2,1)}), bf16[16,64,128]{2,1,0:T(8,128)(2,1)S(1)}, u32[]{:S(2)}, u32[]{:S(2)}) %all-to-all-start) | async-done | bytes 262176 | tf_op jit(solution)/shard_map/all_to_all | solution.py:33
  642.6 11.6 %dynamic_update_slice.97 = bf16[16,512,256]{1,2,0:T(8,128)(2,1)} dynamic-update-slice(bf16[16,512,256]{1,2,0:T(8,128)(2,1)} %dynamic_update_slice.96, bf16[16,64,256]{1,2,0:T(8,128)(2,1)S(1)} %copy.48, s32[]{:T(128)} %constant.97.clone.1, s32[]{:T(128)S(6)} %select_n.133, s32[]{:T(128)} %constant.97.clone.1) | dynamic-update-slice | bytes 1048580 | tf_op jit(solution)/shard_map/dynamic_update_slice | solution.py:17
  654.7 11.5 %dynamic_update_slice.105 = bf16[16,512,256]{1,2,0:T(8,128)(2,1)} dynamic-update-slice(bf16[16,512,256]{1,2,0:T(8,128)(2,1)} %dynamic_update_slice.104, bf16[16,64,256]{1,2,0:T(8,128)(2,1)S(1)} %copy.59, s32[]{:T(128)} %constant.97.clone.1, s32[]{:T(128)S(6)} %select_n.133, s32[]{:T(128)} %constant.97.clone.1) | dynamic-update-slice | bytes 1048580 | tf_op jit(solution)/shard_map/dynamic_update_slice | solution.py:17
  666.7 12.2 %dynamic_update_slice.98 = bf16[16,512,256]{1,2,0:T(8,128)(2,1)} dynamic-update-slice(bf16[16,512,256]{1,2,0:T(8,128)(2,1)} %dynamic_update_slice.97, bf16[16,64,256]{1,2,0:T(8,128)(2,1)S(1)} %copy.49, s32[]{:T(128)} %constant.97.clone.1, s32[]{:T(128)S(6)} %select_n.135, s32[]{:T(128)} %constant.97.clone.1) | dynamic-update-slice | bytes 1048580 | tf_op jit(solution)/shard_map/dynamic_update_slice | solution.py:22
  679.4 12.3 %dynamic_update_slice.106 = bf16[16,512,256]{1,2,0:T(8,128)(2,1)} dynamic-update-slice(bf16[16,512,256]{1,2,0:T(8,128)(2,1)} %dynamic_update_slice.105, bf16[16,64,256]{1,2,0:T(8,128)(2,1)S(1)} %copy.60, s32[]{:T(128)} %constant.97.clone.1, s32[]{:T(128)S(6)} %select_n.135, s32[]{:T(128)} %constant.97.clone.1) | dynamic-update-slice | bytes 1048580 | tf_op jit(solution)/shard_map/dynamic_update_slice | solution.py:22
  692.2 11.5 %dynamic_update_slice.113 = bf16[16,512,256]{1,2,0:T(8,128)(2,1)} dynamic-update-slice(bf16[16,512,256]{1,2,0:T(8,128)(2,1)} %dynamic_update_slice.112, bf16[16,64,256]{1,2,0:T(8,128)(2,1)S(1)} %copy.68, s32[]{:T(128)} %constant.97.clone.1, s32[]{:T(128)S(6)} %select_n.133, s32[]{:T(128)} %constant.97.clone.1) | dynamic-update-slice | bytes 1048580 | tf_op jit(solution)/shard_map/dynamic_update_slice | solution.py:17
  704.2 12.3 %dynamic_update_slice.114 = bf16[16,512,256]{1,2,0:T(8,128)(2,1)} dynamic-update-slice(bf16[16,512,256]{1,2,0:T(8,128)(2,1)} %dynamic_update_slice.113, bf16[16,64,256]{1,2,0:T(8,128)(2,1)S(1)} %copy.69, s32[]{:T(128)} %constant.97.clone.1, s32[]{:T(128)S(6)} %select_n.135, s32[]{:T(128)} %constant.97.clone.1) | dynamic-update-slice | bytes 1048580 | tf_op jit(solution)/shard_map/dynamic_update_slice | solution.py:22
  717.0 11.5 %dynamic_update_slice.121 = bf16[16,512,256]{1,2,0:T(8,128)(2,1)} dynamic-update-slice(bf16[16,512,256]{1,2,0:T(8,128)(2,1)} %dynamic_update_slice.120, bf16[16,64,256]{1,2,0:T(8,128)(2,1)S(1)} %copy.77, s32[]{:T(128)} %constant.97.clone.1, s32[]{:T(128)S(6)} %select_n.133, s32[]{:T(128)} %constant.97.clone.1) | dynamic-update-slice | bytes 1048580 | tf_op jit(solution)/shard_map/dynamic_update_slice | solution.py:17
  729.0 12.2 %dynamic_update_slice.122 = bf16[16,512,256]{1,2,0:T(8,128)(2,1)} dynamic-update-slice(bf16[16,512,256]{1,2,0:T(8,128)(2,1)} %dynamic_update_slice.121, bf16[16,64,256]{1,2,0:T(8,128)(2,1)S(1)} %copy.78, s32[]{:T(128)} %constant.97.clone.1, s32[]{:T(128)S(6)} %select_n.135, s32[]{:T(128)} %constant.97.clone.1) | dynamic-update-slice | bytes 1048580 | tf_op jit(solution)/shard_map/dynamic_update_slice | solution.py:22
  761.5 10.4 dynamic_update_slice.100
  772.4 10.2 dynamic_update_slice.108
  794.0 10.3 dynamic_update_slice.116
  816.7 10.3 dynamic_update_slice.124
  828.6 12.2 %dynamic_update_slice.101 = bf16[16,512,256]{1,2,0:T(8,128)(2,1)} dynamic-update-slice(bf16[16,512,256]{1,2,0:T(8,128)(2,1)} %dynamic_update_slice.100, bf16[16,64,256]{1,2,0:T(8,128)(2,1)S(1)} %copy.52, s32[]{:T(128)} %constant.97.clone.1, s32[]{:T(128)S(6)} %select_n.141, s32[]{:T(128)} %constant.97.clone.1) | dynamic-update-slice | bytes 1048580 | tf_op jit(solution)/shard_map/dynamic_update_slice | solution.py:17
  842.4 12.3 %dynamic_update_slice.109 = bf16[16,512,256]{1,2,0:T(8,128)(2,1)} dynamic-update-slice(bf16[16,512,256]{1,2,0:T(8,128)(2,1)} %dynamic_update_slice.108, bf16[16,64,256]{1,2,0:T(8,128)(2,1)S(1)} %copy.63, s32[]{:T(128)} %constant.97.clone.1, s32[]{:T(128)S(6)} %select_n.141, s32[]{:T(128)} %constant.97.clone.1) | dynamic-update-slice | bytes 1048580 | tf_op jit(solution)/shard_map/dynamic_update_slice | solution.py:17
  855.2 12.2 %dynamic_update_slice.102 = bf16[16,512,256]{1,2,0:T(8,128)(2,1)} dynamic-update-slice(bf16[16,512,256]{1,2,0:T(8,128)(2,1)} %dynamic_update_slice.101, bf16[16,64,256]{1,2,0:T(8,128)(2,1)S(1)} %copy.53, s32[]{:T(128)} %constant.97.clone.1, s32[]{:T(128)S(6)} %select_n.143, s32[]{:T(128)} %constant.97.clone.1) | dynamic-update-slice | bytes 1048580 | tf_op jit(solution)/shard_map/dynamic_update_slice | solution.py:22
  867.9 12.2 %dynamic_update_slice.110 = bf16[16,512,256]{1,2,0:T(8,128)(2,1)} dynamic-update-slice(bf16[16,512,256]{1,2,0:T(8,128)(2,1)} %dynamic_update_slice.109, bf16[16,64,256]{1,2,0:T(8,128)(2,1)S(1)} %copy.64, s32[]{:T(128)} %constant.97.clone.1, s32[]{:T(128)S(6)} %select_n.143, s32[]{:T(128)} %constant.97.clone.1) | dynamic-update-slice | bytes 1048580 | tf_op jit(solution)/shard_map/dynamic_update_slice | solution.py:22
  881.7 12.3 %dynamic_update_slice.117 = bf16[16,512,256]{1,2,0:T(8,128)(2,1)} dynamic-update-slice(bf16[16,512,256]{1,2,0:T(8,128)(2,1)} %dynamic_update_slice.116, bf16[16,64,256]{1,2,0:T(8,128)(2,1)S(1)} %copy.72, s32[]{:T(128)} %constant.97.clone.1, s32[]{:T(128)S(6)} %select_n.141, s32[]{:T(128)} %constant.97.clone.1) | dynamic-update-slice | bytes 1048580 | tf_op jit(solution)/shard_map/dynamic_update_slice | solution.py:17
  895.5 12.3 %dynamic_update_slice.118 = bf16[16,512,256]{1,2,0:T(8,128)(2,1)} dynamic-update-slice(bf16[16,512,256]{1,2,0:T(8,128)(2,1)} %dynamic_update_slice.117, bf16[16,64,256]{1,2,0:T(8,128)(2,1)S(1)} %copy.73, s32[]{:T(128)} %constant.97.clone.1, s32[]{:T(128)S(6)} %select_n.143, s32[]{:T(128)} %constant.97.clone.1) | dynamic-update-slice | bytes 1048580 | tf_op jit(solution)/shard_map/dynamic_update_slice | solution.py:22
  909.3 12.2 %dynamic_update_slice.125 = bf16[16,512,256]{1,2,0:T(8,128)(2,1)} dynamic-update-slice(bf16[16,512,256]{1,2,0:T(8,128)(2,1)} %dynamic_update_slice.124, bf16[16,64,256]{1,2,0:T(8,128)(2,1)S(1)} %copy.81, s32[]{:T(128)} %constant.97.clone.1, s32[]{:T(128)S(6)} %select_n.141, s32[]{:T(128)} %constant.97.clone.1) | dynamic-update-slice | bytes 1048580 | tf_op jit(solution)/shard_map/dynamic_update_slice | solution.py:17
  923.1 12.2 %dynamic_update_slice.126 = bf16[16,512,256]{1,2,0:T(8,128)(2,1)} dynamic-update-slice(bf16[16,512,256]{1,2,0:T(8,128)(2,1)} %dynamic_update_slice.125, bf16[16,64,256]{1,2,0:T(8,128)(2,1)S(1)} %copy.82, s32[]{:T(128)} %constant.97.clone.1, s32[]{:T(128)S(6)} %select_n.143, s32[]{:T(128)} %constant.97.clone.1) | dynamic-update-slice | bytes 1048580 | tf_op jit(solution)/shard_map/dynamic_update_slice | solution.py:22
  943.3 10.5 dynamic_update_slice.103
  958.8 10.3 dynamic_update_slice.111
  981.6 10.3 dynamic_update_slice.119
  1002.8 10.2 dynamic_update_slice.127
  1022.3 16.2 %fusion.24 = f32[2,16,512]{2,1,0:T(8,128)} fusion(bf16[2,16,128,256]{3,1,2,0:T(8,128)(2,1)} %copy.57, bf16[512,128,256]{2,0,1:T(8,128)(2,1)} %all-gather.2.cloned.1.call-done), kind=kOutput, calls=%fused_computation.20 | convolution fusion | flops 1073741824 | bytes 35717120 | tf_op jit(solution)/shard_map/dot_general | solution.py:48
  1038.5 16.0 %fusion.27 = f32[2,16,512]{2,1,0:T(8,128)} fusion(bf16[2,16,128,256]{3,1,2,0:T(8,128)(2,1)S(1)} %copy.66, bf16[512,128,256]{2,0,1:T(8,128)(2,1)} %all-gather.2.cloned.1.call-done), kind=kOutput, calls=%fused_computation.21 | convolution fusion | flops 1073741824 | bytes 35717120 | tf_op jit(solution)/shard_map/dot_general | solution.py:48
  1054.6 16.3 %fusion.30 = f32[2,16,512]{2,1,0:T(8,128)} fusion(bf16[2,16,128,256]{3,1,2,0:T(8,128)(2,1)} %copy.75, bf16[512,128,256]{2,0,1:T(8,128)(2,1)} %all-gather.2.cloned.1.call-done), kind=kOutput, calls=%fused_computation.22 | convolution fusion | flops 1073741824 | bytes 35717120 | tf_op jit(solution)/shard_map/dot_general | solution.py:48
  1071.0 15.8 %fusion.33 = f32[2,16,512]{2,1,0:T(8,128)} fusion(bf16[2,16,128,256]{3,1,2,0:T(8,128)(2,1)S(1)} %copy-done, bf16[512,128,256]{2,0,1:T(8,128)(2,1)} %all-gather.2.cloned.1.call-done), kind=kOutput, calls=%fused_computation.23 | convolution fusion | flops 1073741824 | bytes 35717120 | tf_op jit(solution)/shard_map/dot_general | solution.py:48
  1087.1 21.7 %reduce-scatter.9.cloned.1.call-done = f32[2,16,128]{2,1,0:T(8,128)} async-done(((f32[2,16,512]{2,1,0:T(8,128)}), f32[2,16,128]{2,1,0:T(8,128)}) %reduce-scatter.9.cloned.1.call-update) | async-done | bytes 16400 | tf_op jit(solution)/shard_map/reduce_scatter | solution.py:53
  1108.8 21.9 %reduce-scatter.11.cloned.1.call-done = f32[2,16,128]{2,1,0:T(8,128)} async-done(((f32[2,16,512]{2,1,0:T(8,128)}), f32[2,16,128]{2,1,0:T(8,128)}) %reduce-scatter.11.cloned.1.call-update) | async-done | bytes 16400 | tf_op jit(solution)/shard_map/reduce_scatter | solution.py:53
  (196 shorter events, 242.0 us)
Async XLA Ops:
  6.5 1015.8 %all-gather.2.cloned.1.call-start = ((), (), s32[]{:S(2)}) async-start(), calls=%async_computation.5 | async-start | bytes 37748736 | tf_op jit(solution)/shard_map/all_gather | solution.py:29
  13.2 548.7 %copy-start.37 = (s32[2,2]{1,0:T(2,128)S(1)}, s32[2,2]{1,0:T(2,128)}, u32[]{:S(2)}) copy-start(s32[2,2]{1,0:T(2,128)} %param.9) | copy-start | bytes 52
  15.0 242.4 %copy-start.4 = (bf16[16,64,256]{2,1,0:T(8,128)(2,1)}, bf16[16,64,256]{2,1,0:T(8,128)(2,1)S(1)}, u32[]{:S(2)}) copy-start(bf16[16,64,256]{2,1,0:T(8,128)(2,1)S(1)} %get-tuple-element.12) | copy-start | bytes 1572868
  15.0 551.0 %copy-start.39 = (f32[512]{0:T(512)S(1)}, f32[512]{0:T(512)}, u32[]{:S(2)}) copy-start(f32[512]{0:T(512)} %param.11) | copy-start | bytes 6148
  15.0 97.8 %collective-permute-start = (bf16[16,64,256]{2,1,0:T(8,128)(2,1)S(1)}, bf16[16,64,256]{2,1,0:T(8,128)(2,1)S(1)}, u32[]{:S(2)}, u32[]{:S(2)}) collective-permute-start(bf16[16,64,256]{2,1,0:T(8,128)(2,1)S(1)} %get-tuple-element.9), channel_id=1, source_target_pairs={{0,4},{4,8},{8,12},{12,16},{16,20},{20,24},{24,28},{28,0},{1,5},{5... | collective-permute-start | bytes 1572872 | tf_op jit(solution)/shard_map/ppermute | solution.py:16
  18.0 104.5 %collective-permute-start.1 = (bf16[16,64,256]{2,1,0:T(8,128)(2,1)S(1)}, bf16[16,64,256]{2,1,0:T(8,128)(2,1)S(1)}, u32[]{:S(2)}, u32[]{:S(2)}) collective-permute-start(bf16[16,64,256]{2,1,0:T(8,128)(2,1)S(1)} %get-tuple-element.9), channel_id=1, source_target_pairs={{0,28},{4,0},{8,4},{12,8},{16,12},{20,16},{24,20},{28,24},{1,29},{... | collective-permute-start | bytes 1572872 | tf_op jit(solution)/shard_map/ppermute | solution.py:21
  21.1 136.7 %collective-permute-start.7 = (bf16[16,64,256]{2,1,0:T(8,128)(2,1)S(1)}, bf16[16,64,256]{2,1,0:T(8,128)(2,1)S(1)}, u32[]{:S(2)}, u32[]{:S(2)}) collective-permute-start(bf16[16,64,256]{2,1,0:T(8,128)(2,1)S(1)} %get-tuple-element.10), channel_id=1, source_target_pairs={{0,4},{4,8},{8,12},{12,16},{16,20},{20,24},{24,28},{28,0},{1,5},{5... | collective-permute-start | bytes 1572872 | tf_op jit(solution)/shard_map/ppermute | solution.py:16
  21.1 146.4 %collective-permute-start.8 = (bf16[16,64,256]{2,1,0:T(8,128)(2,1)S(1)}, bf16[16,64,256]{2,1,0:T(8,128)(2,1)S(1)}, u32[]{:S(2)}, u32[]{:S(2)}) collective-permute-start(bf16[16,64,256]{2,1,0:T(8,128)(2,1)S(1)} %get-tuple-element.10), channel_id=1, source_target_pairs={{0,28},{4,0},{8,4},{12,8},{16,12},{20,16},{24,20},{28,24},{1,29},{... | collective-permute-start | bytes 1572872 | tf_op jit(solution)/shard_map/ppermute | solution.py:21
  25.9 176.9 %collective-permute-start.14 = (bf16[16,64,256]{2,1,0:T(8,128)(2,1)S(1)}, bf16[16,64,256]{2,1,0:T(8,128)(2,1)S(1)}, u32[]{:S(2)}, u32[]{:S(2)}) collective-permute-start(bf16[16,64,256]{2,1,0:T(8,128)(2,1)S(1)} %get-tuple-element.12), channel_id=1, source_target_pairs={{0,4},{4,8},{8,12},{12,16},{16,20},{20,24},{24,28},{28,0},{1,5},{5... | collective-permute-start | bytes 1572872 | tf_op jit(solution)/shard_map/ppermute | solution.py:16
  112.9 279.4 %copy-start.14 = (bf16[16,64,256]{2,1,0:T(8,128)(2,1)}, bf16[16,64,256]{2,1,0:T(8,128)(2,1)S(1)}, u32[]{:S(2)}) copy-start(bf16[16,64,256]{2,1,0:T(8,128)(2,1)S(1)} %collective-permute-done) | copy-start | bytes 1572868
  112.9 99.6 %collective-permute-start.15 = (bf16[16,64,256]{2,1,0:T(8,128)(2,1)S(1)}, bf16[16,64,256]{2,1,0:T(8,128)(2,1)S(1)}, u32[]{:S(2)}, u32[]{:S(2)}) collective-permute-start(bf16[16,64,256]{2,1,0:T(8,128)(2,1)S(1)} %get-tuple-element.12), channel_id=1, source_target_pairs={{0,28},{4,0},{8,4},{12,8},{16,12},{20,16},{24,20},{28,24},{1,29},{... | collective-permute-start | bytes 1572872 | tf_op jit(solution)/shard_map/ppermute | solution.py:21
  122.6 441.5 %copy-start.6 = (bf16[16,64,256]{2,1,0:T(8,128)(2,1)}, bf16[16,64,256]{2,1,0:T(8,128)(2,1)S(1)}, u32[]{:S(2)}) copy-start(bf16[16,64,256]{2,1,0:T(8,128)(2,1)S(1)} %collective-permute-done.1) | copy-start | bytes 1572868
  122.6 125.1 %collective-permute-start.21 = (bf16[16,64,256]{2,1,0:T(8,128)(2,1)S(1)}, bf16[16,64,256]{2,1,0:T(8,128)(2,1)S(1)}, u32[]{:S(2)}, u32[]{:S(2)}) collective-permute-start(bf16[16,64,256]{2,1,0:T(8,128)(2,1)S(1)} %get-tuple-element.11), channel_id=1, source_target_pairs={{0,4},{4,8},{8,12},{12,16},{16,20},{20,24},{24,28},{28,0},{1,5},{5... | collective-permute-start | bytes 1572872 | tf_op jit(solution)/shard_map/ppermute | solution.py:16
  157.8 354.0 %copy-start.22 = (bf16[16,64,256]{2,1,0:T(8,128)(2,1)}, bf16[16,64,256]{2,1,0:T(8,128)(2,1)S(1)}, u32[]{:S(2)}) copy-start(bf16[16,64,256]{2,1,0:T(8,128)(2,1)S(1)} %collective-permute-done.7) | copy-start | bytes 1572868
  157.8 99.6 %collective-permute-start.22 = (bf16[16,64,256]{2,1,0:T(8,128)(2,1)S(1)}, bf16[16,64,256]{2,1,0:T(8,128)(2,1)S(1)}, u32[]{:S(2)}, u32[]{:S(2)}) collective-permute-start(bf16[16,64,256]{2,1,0:T(8,128)(2,1)S(1)} %get-tuple-element.11), channel_id=1, source_target_pairs={{0,28},{4,0},{8,4},{12,8},{16,12},{20,16},{24,20},{28,24},{1,29},{... | collective-permute-start | bytes 1572872 | tf_op jit(solution)/shard_map/ppermute | solution.py:21
  167.5 215.0 %copy-start.10 = (bf16[16,64,256]{2,1,0:T(8,128)(2,1)}, bf16[16,64,256]{2,1,0:T(8,128)(2,1)S(1)}, u32[]{:S(2)}) copy-start(bf16[16,64,256]{2,1,0:T(8,128)(2,1)S(1)} %collective-permute-done.8) | copy-start | bytes 1572868
  167.5 125.1 %collective-permute-start.2 = (bf16[16,64,256]{2,1,0:T(8,128)(2,1)S(1)}, bf16[16,64,256]{2,1,0:T(8,128)(2,1)S(1)}, u32[]{:S(2)}, u32[]{:S(2)}) collective-permute-start(bf16[16,64,256]{2,1,0:T(8,128)(2,1)S(1)} %collective-permute-done), channel_id=1, source_target_pairs={{0,4},{4,8},{8,12},{12,16},{16,20},{20,24},{24,28},{28,0},{1,5},{5... | collective-permute-start | bytes 1572872 | tf_op jit(solution)/shard_map/ppermute | solution.py:16
  202.8 99.6 %collective-permute-start.3 = (bf16[16,64,256]{2,1,0:T(8,128)(2,1)S(1)}, bf16[16,64,256]{2,1,0:T(8,128)(2,1)S(1)}, u32[]{:S(2)}, u32[]{:S(2)}) collective-permute-start(bf16[16,64,256]{2,1,0:T(8,128)(2,1)S(1)} %collective-permute-done.1), channel_id=1, source_target_pairs={{0,28},{4,0},{8,4},{12,8},{16,12},{20,16},{24,20},{28,24},{1,29},{... | collective-permute-start | bytes 1572872 | tf_op jit(solution)/shard_map/ppermute | solution.py:21
  212.4 125.1 %collective-permute-start.9 = (bf16[16,64,256]{2,1,0:T(8,128)(2,1)S(1)}, bf16[16,64,256]{2,1,0:T(8,128)(2,1)S(1)}, u32[]{:S(2)}, u32[]{:S(2)}) collective-permute-start(bf16[16,64,256]{2,1,0:T(8,128)(2,1)S(1)} %collective-permute-done.7), channel_id=1, source_target_pairs={{0,4},{4,8},{8,12},{12,16},{16,20},{20,24},{24,28},{28,0},{1,5},{5... | collective-permute-start | bytes 1572872 | tf_op jit(solution)/shard_map/ppermute | solution.py:16
  247.7 234.4 %copy-start.18 = (bf16[16,64,256]{2,1,0:T(8,128)(2,1)}, bf16[16,64,256]{2,1,0:T(8,128)(2,1)S(1)}, u32[]{:S(2)}) copy-start(bf16[16,64,256]{2,1,0:T(8,128)(2,1)S(1)} %collective-permute-done.21) | copy-start | bytes 1572868
  247.7 99.6 %collective-permute-start.10 = (bf16[16,64,256]{2,1,0:T(8,128)(2,1)S(1)}, bf16[16,64,256]{2,1,0:T(8,128)(2,1)S(1)}, u32[]{:S(2)}, u32[]{:S(2)}) collective-permute-start(bf16[16,64,256]{2,1,0:T(8,128)(2,1)S(1)} %collective-permute-done.8), channel_id=1, source_target_pairs={{0,28},{4,0},{8,4},{12,8},{16,12},{20,16},{24,20},{28,24},{1,29},{... | collective-permute-start | bytes 1572872 | tf_op jit(solution)/shard_map/ppermute | solution.py:21
  257.4 224.7 %copy-start.20 = (bf16[16,64,256]{2,1,0:T(8,128)(2,1)}, bf16[16,64,256]{2,1,0:T(8,128)(2,1)S(1)}, u32[]{:S(2)}) copy-start(bf16[16,64,256]{2,1,0:T(8,128)(2,1)S(1)} %collective-permute-done.22) | copy-start | bytes 1572868
  257.4 125.1 %collective-permute-start.16 = (bf16[16,64,256]{2,1,0:T(8,128)(2,1)S(1)}, bf16[16,64,256]{2,1,0:T(8,128)(2,1)S(1)}, u32[]{:S(2)}, u32[]{:S(2)}) collective-permute-start(bf16[16,64,256]{2,1,0:T(8,128)(2,1)S(1)} %collective-permute-done.14), channel_id=1, source_target_pairs={{0,4},{4,8},{8,12},{12,16},{16,20},{20,24},{24,28},{28,0},{1,5},{5... | collective-permute-start | bytes 1572872 | tf_op jit(solution)/shard_map/ppermute | solution.py:16
  257.4 306.6 %copy-start.5 = (bf16[16,64,256]{2,1,0:T(8,128)(2,1)S(1)}, bf16[16,64,256]{2,1,0:T(8,128)(2,1)}, u32[]{:S(2)}) copy-start(bf16[16,64,256]{2,1,0:T(8,128)(2,1)} %copy-done.4) | copy-start | bytes 1572868
  292.6 224.6 %copy-start.24 = (bf16[16,64,256]{2,1,0:T(8,128)(2,1)}, bf16[16,64,256]{2,1,0:T(8,128)(2,1)S(1)}, u32[]{:S(2)}) copy-start(bf16[16,64,256]{2,1,0:T(8,128)(2,1)S(1)} %collective-permute-done.2) | copy-start | bytes 1572868
  292.6 99.7 %collective-permute-start.17 = (bf16[16,64,256]{2,1,0:T(8,128)(2,1)S(1)}, bf16[16,64,256]{2,1,0:T(8,128)(2,1)}, u32[]{:S(2)}, u32[]{:S(2)}) collective-permute-start(bf16[16,64,256]{2,1,0:T(8,128)(2,1)S(1)} %collective-permute-done.15), channel_id=1, source_target_pairs={{0,28},{4,0},{8,4},{12,8},{16,12},{20,16},{24,20},{28,24},{1,29},{... | collective-permute-start | bytes 1572872 | tf_op jit(solution)/shard_map/ppermute | solution.py:21
  302.3 125.1 %collective-permute-start.23 = (bf16[16,64,256]{2,1,0:T(8,128)(2,1)S(1)}, bf16[16,64,256]{2,1,0:T(8,128)(2,1)}, u32[]{:S(2)}, u32[]{:S(2)}) collective-permute-start(bf16[16,64,256]{2,1,0:T(8,128)(2,1)S(1)} %collective-permute-done.21), channel_id=1, source_target_pairs={{0,4},{4,8},{8,12},{12,16},{16,20},{20,24},{24,28},{28,0},{1,5},{5... | collective-permute-start | bytes 1572872 | tf_op jit(solution)/shard_map/ppermute | solution.py:16
  337.6 224.5 %copy-start.30 = (bf16[16,64,256]{2,1,0:T(8,128)(2,1)}, bf16[16,64,256]{2,1,0:T(8,128)(2,1)S(1)}, u32[]{:S(2)}) copy-start(bf16[16,64,256]{2,1,0:T(8,128)(2,1)S(1)} %collective-permute-done.9) | copy-start | bytes 1572868
  337.6 99.7 %collective-permute-start.24 = (bf16[16,64,256]{2,1,0:T(8,128)(2,1)S(1)}, bf16[16,64,256]{2,1,0:T(8,128)(2,1)}, u32[]{:S(2)}, u32[]{:S(2)}) collective-permute-start(bf16[16,64,256]{2,1,0:T(8,128)(2,1)S(1)} %collective-permute-done.22), channel_id=1, source_target_pairs={{0,28},{4,0},{8,4},{12,8},{16,12},{20,16},{24,20},{28,24},{1,29},{... | collective-permute-start | bytes 1572872 | tf_op jit(solution)/shard_map/ppermute | solution.py:21
  347.3 179.8 %copy-start.26 = (bf16[16,64,256]{2,1,0:T(8,128)(2,1)}, bf16[16,64,256]{2,1,0:T(8,128)(2,1)S(1)}, u32[]{:S(2)}) copy-start(bf16[16,64,256]{2,1,0:T(8,128)(2,1)S(1)} %collective-permute-done.10) | copy-start | bytes 1572868
  347.3 119.6 %collective-permute-start.4 = (bf16[16,64,256]{2,1,0:T(8,128)(2,1)S(1)}, bf16[16,64,256]{2,1,0:T(8,128)(2,1)}, u32[]{:S(2)}, u32[]{:S(2)}) collective-permute-start(bf16[16,64,256]{2,1,0:T(8,128)(2,1)S(1)} %collective-permute-done.2), channel_id=1, source_target_pairs={{0,4},{4,8},{8,12},{12,16},{16,20},{20,24},{24,28},{28,0},{1,5},{5... | collective-permute-start | bytes 1572872 | tf_op jit(solution)/shard_map/ppermute | solution.py:16
  382.5 179.6 %copy-start.28 = (bf16[16,64,256]{2,1,0:T(8,128)(2,1)}, bf16[16,64,256]{2,1,0:T(8,128)(2,1)S(1)}, u32[]{:S(2)}) copy-start(bf16[16,64,256]{2,1,0:T(8,128)(2,1)S(1)} %collective-permute-done.16) | copy-start | bytes 1572868
  382.5 99.6 %collective-permute-start.5 = (bf16[16,64,256]{2,1,0:T(8,128)(2,1)S(1)}, bf16[16,64,256]{2,1,0:T(8,128)(2,1)S(1)}, u32[]{:S(2)}, u32[]{:S(2)}) collective-permute-start(bf16[16,64,256]{2,1,0:T(8,128)(2,1)S(1)} %collective-permute-done.3), channel_id=1, source_target_pairs={{0,28},{4,0},{8,4},{12,8},{16,12},{20,16},{24,20},{28,24},{1,29},{... | collective-permute-start | bytes 1572872 | tf_op jit(solution)/shard_map/ppermute | solution.py:21
  392.3 119.5 %collective-permute-start.11 = (bf16[16,64,256]{2,1,0:T(8,128)(2,1)S(1)}, bf16[16,64,256]{2,1,0:T(8,128)(2,1)}, u32[]{:S(2)}, u32[]{:S(2)}) collective-permute-start(bf16[16,64,256]{2,1,0:T(8,128)(2,1)S(1)} %collective-permute-done.9), channel_id=1, source_target_pairs={{0,4},{4,8},{8,12},{12,16},{16,20},{20,24},{24,28},{28,0},{1,5},{5... | collective-permute-start | bytes 1572872 | tf_op jit(solution)/shard_map/ppermute | solution.py:16
  427.5 99.6 %collective-permute-start.12 = (bf16[16,64,256]{2,1,0:T(8,128)(2,1)S(1)}, bf16[16,64,256]{2,1,0:T(8,128)(2,1)S(1)}, u32[]{:S(2)}, u32[]{:S(2)}) collective-permute-start(bf16[16,64,256]{2,1,0:T(8,128)(2,1)S(1)} %collective-permute-done.10), channel_id=1, source_target_pairs={{0,28},{4,0},{8,4},{12,8},{16,12},{20,16},{24,20},{28,24},{1,29},{... | collective-permute-start | bytes 1572872 | tf_op jit(solution)/shard_map/ppermute | solution.py:21
  437.3 122.0 %collective-permute-start.18 = (bf16[16,64,256]{2,1,0:T(8,128)(2,1)S(1)}, bf16[16,64,256]{2,1,0:T(8,128)(2,1)}, u32[]{:S(2)}, u32[]{:S(2)}) collective-permute-start(bf16[16,64,256]{2,1,0:T(8,128)(2,1)S(1)} %collective-permute-done.16), channel_id=1, source_target_pairs={{0,4},{4,8},{8,12},{12,16},{16,20},{20,24},{24,28},{28,0},{1,5},{5... | collective-permute-start | bytes 1572872 | tf_op jit(solution)/shard_map/ppermute | solution.py:16
  466.8 427.1 %collective-permute-start.19 = (bf16[16,64,256]{2,1,0:T(8,128)(2,1)}, bf16[16,64,256]{2,1,0:T(8,128)(2,1)}, u32[]{:S(2)}, u32[]{:S(2)}) collective-permute-start(bf16[16,64,256]{2,1,0:T(8,128)(2,1)} %collective-permute-done.17), channel_id=1, source_target_pairs={{0,28},{4,0},{8,4},{12,8},{16,12},{20,16},{24,20},{28,24},{1,29},{... | collective-permute-start | bytes 1572872 | tf_op jit(solution)/shard_map/ppermute | solution.py:21
  482.1 425.6 %collective-permute-start.25 = (bf16[16,64,256]{2,1,0:T(8,128)(2,1)}, bf16[16,64,256]{2,1,0:T(8,128)(2,1)}, u32[]{:S(2)}, u32[]{:S(2)}) collective-permute-start(bf16[16,64,256]{2,1,0:T(8,128)(2,1)} %collective-permute-done.23), channel_id=1, source_target_pairs={{0,4},{4,8},{8,12},{12,16},{16,20},{20,24},{24,28},{28,0},{1,5},{5... | collective-permute-start | bytes 1572872 | tf_op jit(solution)/shard_map/ppermute | solution.py:16
  511.8 409.7 %collective-permute-start.26 = (bf16[16,64,256]{2,1,0:T(8,128)(2,1)}, bf16[16,64,256]{2,1,0:T(8,128)(2,1)}, u32[]{:S(2)}, u32[]{:S(2)}) collective-permute-start(bf16[16,64,256]{2,1,0:T(8,128)(2,1)} %collective-permute-done.24), channel_id=1, source_target_pairs={{0,28},{4,0},{8,4},{12,8},{16,12},{20,16},{24,20},{28,24},{1,29},{... | collective-permute-start | bytes 1572872 | tf_op jit(solution)/shard_map/ppermute | solution.py:21
  527.8 414.0 %collective-permute-start.6 = (bf16[16,64,256]{2,1,0:T(8,128)(2,1)}, bf16[16,64,256]{2,1,0:T(8,128)(2,1)}, u32[]{:S(2)}, u32[]{:S(2)}) collective-permute-start(bf16[16,64,256]{2,1,0:T(8,128)(2,1)} %collective-permute-done.4), channel_id=1, source_target_pairs={{0,4},{4,8},{8,12},{12,16},{16,20},{20,24},{24,28},{28,0},{1,5},{5... | collective-permute-start | bytes 1572872 | tf_op jit(solution)/shard_map/ppermute | solution.py:16
  527.8 113.6 %all-to-all-start = ((bf16[16,64,128]{2,1,0:T(8,128)(2,1)}), bf16[16,64,128]{2,1,0:T(8,128)(2,1)S(1)}, u32[]{:S(2)}, u32[]{:S(2)}) async-start(bf16[16,64,128]{2,1,0:T(8,128)(2,1)} %param.6), calls=%async_computation | async-start | bytes 524288 | tf_op jit(solution)/shard_map/all_to_all | solution.py:33
  543.9 542.9 %reduce-scatter.5.cloned.1.call-start = ((), (), s32[]{:S(2)}) async-start(), calls=%async_computation.6 | async-start | bytes 81920 | tf_op jit(solution)/shard_map/reduce_scatter | solution.py:53
  559.3 398.0 %collective-permute-start.13 = (bf16[16,64,256]{2,1,0:T(8,128)(2,1)}, bf16[16,64,256]{2,1,0:T(8,128)(2,1)}, u32[]{:S(2)}, u32[]{:S(2)}) collective-permute-start(bf16[16,64,256]{2,1,0:T(8,128)(2,1)} %collective-permute-done.11), channel_id=1, source_target_pairs={{0,4},{4,8},{8,12},{12,16},{16,20},{20,24},{24,28},{28,0},{1,5},{5... | collective-permute-start | bytes 1572872 | tf_op jit(solution)/shard_map/ppermute | solution.py:16
  935.3 44.8 %collective-permute-start.20 = (bf16[16,64,256]{2,1,0:T(8,128)(2,1)}, bf16[16,64,256]{2,1,0:T(8,128)(2,1)}, u32[]{:S(2)}, u32[]{:S(2)}) collective-permute-start(bf16[16,64,256]{2,1,0:T(8,128)(2,1)} %collective-permute-done.18), channel_id=1, source_target_pairs={{0,4},{4,8},{8,12},{12,16},{16,20},{20,24},{24,28},{28,0},{1,5},{5... | collective-permute-start | bytes 1572872 | tf_op jit(solution)/shard_map/ppermute | solution.py:16
  935.3 65.9 %collective-permute-start.27 = (bf16[16,64,256]{2,1,0:T(8,128)(2,1)}, bf16[16,64,256]{2,1,0:T(8,128)(2,1)}, u32[]{:S(2)}, u32[]{:S(2)}) collective-permute-start(bf16[16,64,256]{2,1,0:T(8,128)(2,1)} %collective-permute-done.25), channel_id=1, source_target_pairs={{0,4},{4,8},{8,12},{12,16},{16,20},{20,24},{24,28},{28,0},{1,5},{5... | collective-permute-start | bytes 1572872 | tf_op jit(solution)/shard_map/ppermute | solution.py:16
  1038.5 48.6 %reduce-scatter.7.cloned.1.call-start = ((), (), s32[]{:S(2)}) async-start(), calls=%async_computation.7 | async-start | bytes 81920 | tf_op jit(solution)/shard_map/reduce_scatter | solution.py:53
  1054.5 54.3 %reduce-scatter.9.cloned.1.call-start = ((), (), s32[]{:S(2)}) async-start(), calls=%async_computation.8 | async-start | bytes 81920 | tf_op jit(solution)/shard_map/reduce_scatter | solution.py:53
  1070.9 59.8 %reduce-scatter.11.cloned.1.call-start = ((), (), s32[]{:S(2)}) async-start(), calls=%async_computation.9 | async-start | bytes 81920 | tf_op jit(solution)/shard_map/reduce_scatter | solution.py:53
  (27 other events, 1061.5 us)
Sparse Core Ops, SparseCore 0:
  13.3 953.9 all-gather.1
  1038.6 26.2 reduce-scatter.4
  1067.5 19.5 reduce-scatter.6
  1089.3 19.4 reduce-scatter.8
  1111.2 19.4 reduce-scatter.10
